TPU v7x, 512 devices: a whole 4x4x16 slice. The times are simulated.
512 devices in a mesh: wa: 32 (over x, y, core), ha: 16 (over z).
Axes of the slice: x: 4, y: 4, z: 16, core: 2. Of those that a mesh axis runs over, the one named last changes fastest.
Arguments:
- residual_in: bfloat16 [192, 16384], P('ha', 'wa'), may hold values from -43.25 to 43.25
- grad_out: bfloat16 [192, 16384], P('ha', 'wa'), may hold values from -6 to 6
- norm_gain: bfloat16 [16384], P('wa'), may hold values from 0.099609375 to 1.8984375
- w_gate: bfloat16 [16384, 26624], P('wa', 'ha'), may hold values from -0.0390625 to 0.0390625
- w_up: bfloat16 [16384, 26624], P('wa', 'ha'), may hold values from -0.0390625 to 0.0390625
- w_down: bfloat16 [26624, 16384], P('ha', 'wa'), may hold values from -0.030643146 to 0.030643146
Outputs:
- grad_in: bfloat16 [192, 16384], P('ha', 'wa')
All inputs are finite; a program needn't handle non-finite values.
Results may differ from a plain program's by a relative error of at most 0.0053.
Values may be sent and summed in bfloat16 or wider, within the bound.
No kernel may reach another device: no remote copies, remote signals or barrier semaphores. Data moves between devices by JAX's collectives and lax.ppermute only.
A program may use at most 64 MiB of HBM per device.

v0:
```python
import jax
import jax.numpy as jnp
from jax import lax
from jax.sharding import PartitionSpec as P

D = 16384


def gate_grads(gate, up, d_hidden):
    sig = jax.nn.sigmoid(gate)
    d_up = (d_hidden * gate * sig).astype(jnp.bfloat16)
    d_gate = (d_hidden * up * sig * (1.0 + gate * (1.0 - sig))).astype(jnp.bfloat16)
    return jnp.stack([d_gate, d_up])


def local(residual_in, grad_out, norm_gain, w_gate, w_up, w_down):
    stream = residual_in.astype(jnp.float32)
    squares = lax.psum(jnp.sum(stream * stream, axis=1), "wa")
    inv_rms = lax.rsqrt(squares / D + 1e-05)[:, None]
    gain_f = norm_gain.astype(jnp.float32)
    normed = (stream * inv_rms * gain_f).astype(jnp.bfloat16)
    stacked = jnp.stack([normed, grad_out])
    piece = lax.all_gather(stacked, "ha", axis=1, tiled=True)
    gate_part = jnp.dot(piece[0], w_gate, preferred_element_type=jnp.float32)
    up_part = jnp.dot(piece[0], w_up, preferred_element_type=jnp.float32)
    back_part = lax.dot_general(
        piece[1], w_down, (((1,), (1,)), ((), ())), preferred_element_type=jnp.float32
    )
    partial_sums = jnp.stack([gate_part, up_part, back_part])
    summed = lax.psum(partial_sums, "wa")
    grads = gate_grads(summed[0], summed[1], summed[2])
    total = lax.dot_general(
        grads[0], w_gate, (((1,), (1,)), ((), ())), preferred_element_type=jnp.float32
    )
    d_normed = lax.psum_scatter(
        total
        + lax.dot_general(
            grads[1], w_up, (((1,), (1,)), ((), ())), preferred_element_type=jnp.float32
        ),
        "ha",
        scatter_dimension=0,
        tiled=True,
    )
    scaled = d_normed * gain_f
    row_dot = lax.psum(jnp.sum(scaled * stream, axis=1), "wa")[:, None]
    grad_in = grad_out.astype(jnp.float32) + inv_rms * scaled - stream * inv_rms**3 * row_dot / D
    return grad_in.astype(jnp.bfloat16)


def solution(mesh):
    placed = (P("ha", "wa"), P("ha", "wa"), P("wa"), P("wa", "ha"), P("wa", "ha"), P("ha", "wa"))
    return jax.shard_map(
        local, mesh=mesh, in_specs=placed, out_specs=P("ha", "wa"), check_vma=False
    )
```

profile of v0, /device:TPU:1, one launch (start us, length us, event | category | flops | bytes accessed | tf_op | source)
XLA Modules:
  0.0 384.8 jit_solution(6059536915146214695)
XLA Ops:
  6.5 1.0 fusion.8
  7.5 69.0 %psum.21 = f32[12]{0:T(128)S(1)} all-reduce(f32[12]{0:T(128)S(1)} %fusion.8), channel_id=1, replica_groups=mesh['wa'=32,'ha'=16] {'wa'}, use_global_device_ids=true, to_apply=%region_1.0 | all-reduce | flops 12 | bytes 96 | tf_op jit(solution)/shard_map/psum | solution.py:18
  76.5 0.7 convert_element_type.23
  77.2 0.8 fusion.16
  78.0 0.7 pad_maximum_fusion.1
  78.8 25.4 %all_gather.3 = bf16[2,192,512]{2,0,1:T(2,128)(2,1)S(1)} all-gather(bf16[2,12,512]{2,0,1:T(2,128)(2,1)S(1)} %copy.7), channel_id=1, replica_groups=mesh['wa'=32,'ha'=16] {'ha'}, dimensions={1}, use_global_device_ids=true | all-gather | bytes 417792 | tf_op jit(solution)/shard_map/all_gather | solution.py:23
  104.2 0.5 fusion.19
  104.7 0.5 convolution_bitcast_fusion.1
  105.3 0.5 convolution_bitcast_fusion.2
  105.8 0.9 copy-done.1
  106.7 0.7 convolution_bitcast_fusion
  107.4 2.1 pad_maximum_fusion
  109.6 143.8 %all-reduce.4.cloned.1.call-done = f32[3,192,1664]{2,1,0:T(8,128)} async-done(((f32[3,192,1664]{2,1,0:T(8,128)}), f32[3,192,1664]{2,1,0:T(8,128)}) %all-reduce.4.cloned.1.call-update) | async-done | bytes 3833872 | tf_op jit(solution)/shard_map/psum | solution.py:30
  253.4 2.8 fusion.6
  256.2 3.2 convolution_add_fusion
  259.5 29.2 %fusion = f32[16,512]{1,0:T(8,128)S(1)} fusion(f32[192,512]{1,0:T(8,128)} %convolution_add_fusion), kind=kCustom, calls=%all-reduce-scatter | all-reduce-scatter fusion | flops 131073 | bytes 428032
  288.7 1.7 collective-permute-start
  290.4 2.7 collective-permute-start.1
  293.2 4.9 %collective-permute-start.2 = (f32[16,512]{1,0:T(8,128)S(1)}, f32[16,512]{1,0:T(8,128)S(1)}, u32[]{:S(2)}, u32[]{:S(2)}) collective-permute-start(f32[16,512]{1,0:T(8,128)S(1)} %fusion), channel_id=1, source_target_pairs={{0,3},{1,4},{2,5},{3,6},{4,7},{5,8},{6,9},{7,10},{8,11},{9,12},{10... | collective-permute-start | bytes 98312
  298.1 5.6 %collective-permute-start.3 = (f32[12,512]{1,0:T(8,128)S(1)}, f32[12,512]{1,0:T(8,128)S(1)}, u32[]{:S(2)}, u32[]{:S(2)}) collective-permute-start(f32[12,512]{1,0:T(8,128)S(1)} %slice.26), channel_id=1, source_target_pairs={{0,4},{1,5},{2,6},{3,7},{4,8},{5,9},{6,10},{7,11},{8,12},{9,13},{1... | collective-permute-start | bytes 73736
  303.7 1.3 dynamic-slice.4
  305.6 0.5 concatenate
  306.3 71.0 %psum.23 = f32[12]{0:T(128)S(1)} all-reduce(f32[12]{0:T(128)S(1)} %fusion.15), channel_id=1, replica_groups=mesh['wa'=32,'ha'=16] {'wa'}, use_global_device_ids=true, to_apply=%region_5.0 | all-reduce | flops 12 | bytes 96 | tf_op jit(solution)/shard_map/psum | solution.py:45
  377.3 0.7 fusion.14
  (19 shorter events, 0.2 us)
Async XLA Ops:
  6.5 98.7 %copy-start = (bf16[512,1664]{1,0:T(8,128)(2,1)S(1)}, bf16[512,1664]{1,0:T(8,128)(2,1)}, u32[]{:S(2)}) copy-start(bf16[512,1664]{1,0:T(8,128)(2,1)} %param.9) | copy-start | bytes 5111812
  6.5 98.2 %copy-start.2 = (bf16[512,1664]{1,0:T(8,128)(2,1)S(1)}, bf16[512,1664]{1,0:T(8,128)(2,1)}, u32[]{:S(2)}) copy-start(bf16[512,1664]{1,0:T(8,128)(2,1)} %param.10) | copy-start | bytes 5111812
  6.5 246.9 %all-reduce.4.cloned.1.call-start = ((), (), s32[]{:S(2)}) async-start(), calls=%async_computation | async-start | bytes 7667712 | tf_op jit(solution)/shard_map/psum | solution.py:30
  105.3 1.5 copy-start.1
  256.2 50.0 %copy-start.3 = (bf16[12,512]{1,0:T(8,128)(2,1)S(1)}, bf16[12,512]{1,0:T(8,128)(2,1)}, u32[]{:S(2)}) copy-start(bf16[12,512]{1,0:T(8,128)(2,1)} %param.6) | copy-start | bytes 36868
  256.2 121.0 %copy-start.4 = (bf16[12,512]{1,0:T(8,128)(2,1)S(1)}, bf16[12,512]{1,0:T(8,128)(2,1)}, u32[]{:S(2)}) copy-start(bf16[12,512]{1,0:T(8,128)(2,1)} %param.7) | copy-start | bytes 36868
  288.7 16.9 %collective-permute-start = (f32[16,512]{1,0:T(8,128)S(1)}, f32[16,512]{1,0:T(8,128)S(1)}, u32[]{:S(2)}, u32[]{:S(2)}) collective-permute-start(f32[16,512]{1,0:T(8,128)S(1)} %fusion), channel_id=1, source_target_pairs={{0,1},{1,2},{2,3},{3,4},{4,5},{5,6},{6,7},{7,8},{8,9},{9,10},{10,1... | collective-permute-start | bytes 98312
  290.4 15.2 %collective-permute-start.1 = (f32[16,512]{1,0:T(8,128)S(1)}, f32[16,512]{1,0:T(8,128)S(1)}, u32[]{:S(2)}, u32[]{:S(2)}) collective-permute-start(f32[16,512]{1,0:T(8,128)S(1)} %fusion), channel_id=1, source_target_pairs={{0,2},{1,3},{2,4},{3,5},{4,6},{5,7},{6,8},{7,9},{8,10},{9,11},{10,... | collective-permute-start | bytes 98312
  293.2 12.5 %collective-permute-start.2 = (f32[16,512]{1,0:T(8,128)S(1)}, f32[16,512]{1,0:T(8,128)S(1)}, u32[]{:S(2)}, u32[]{:S(2)}) collective-permute-start(f32[16,512]{1,0:T(8,128)S(1)} %fusion), channel_id=1, source_target_pairs={{0,3},{1,4},{2,5},{3,6},{4,7},{5,8},{6,9},{7,10},{8,11},{9,12},{10... | collective-permute-start | bytes 98312
  298.1 7.5 %collective-permute-start.3 = (f32[12,512]{1,0:T(8,128)S(1)}, f32[12,512]{1,0:T(8,128)S(1)}, u32[]{:S(2)}, u32[]{:S(2)}) collective-permute-start(f32[12,512]{1,0:T(8,128)S(1)} %slice.26), channel_id=1, source_target_pairs={{0,4},{1,5},{2,6},{3,7},{4,8},{5,9},{6,10},{7,11},{8,12},{9,13},{1... | collective-permute-start | bytes 73736
Sparse Core Ops, SparseCore 0:
  109.7 143.6 all-reduce.3
where the time goes:
time: 385 us
  blocking collectives  195 us (51%)
  waiting for transfers between devices  144 us (37%)
  starting transfers between devices  14.9 us (4%)
  between operations  14.2 us (4%)
  matrix products  7.8 us (2%)
  other arithmetic  6.15 us (2%)
    psum x1, waiting for transfers between devices, local(): summed = lax.psum(partial_sums, 'wa')  144 us
    psum x1, blocking collectives, local(): row_dot = lax.psum(jnp.sum(scaled * stream, axis=1), 'wa')[:, None]  71 us
    psum x1, blocking collectives, local(): squares = lax.psum(jnp.sum(stream * stream, axis=1), 'wa')  69 us
    unnamed x1, blocking collectives  29.2 us
    all_gather x1, blocking collectives, local(): piece = lax.all_gather(stacked, 'ha', axis=1, tiled=True)  25.4 us
    unnamed x4, starting transfers between devices  14.9 us
  transfers between devices with their start and end apart: 5, of which 1 were waited for; matrix products, arithmetic and copies ran while one was open for 0% of the time, Pallas kernels for 0%

commit v1 on v0

--- a/solution.py
+++ b/solution.py
@@ -20,7 +20,40 @@
     gain_f = norm_gain.astype(jnp.float32)
     normed = (stream * inv_rms * gain_f).astype(jnp.bfloat16)
     stacked = jnp.stack([normed, grad_out])
-    piece = lax.all_gather(stacked, "ha", axis=1, tiled=True)
+
+    def _post_trees(z_in, net_axis):
+        t_next = jax.lax.axis_size(net_axis)
+        local_part = jax.lax.axis_index(net_axis)
+        arr_out, b_next, clean = (t_next, local_part, z_in.shape[1])
+        chunks = []
+        j0 = 0
+        while j0 < arr_out:
+            chunks.append((j0, (j0 + 1) % arr_out))
+            j0 += 1
+        leaves = []
+        j0 = 0
+        while j0 < arr_out:
+            leaves.append((j0, (j0 - 1) % arr_out))
+            j0 += 1
+        m_next = jnp.zeros((*z_in.shape[:1], arr_out * clean, *z_in.shape[2:]), z_in.dtype)
+        m_next = lax.dynamic_update_slice_in_dim(m_next, z_in, b_next * clean, axis=1)
+        val2 = block_last = z_in
+        y2 = arr_out // 2
+        kk = 1
+        while kk < y2 + 1:
+            val2 = jax.lax.ppermute(val2, net_axis, chunks)
+            m_next = lax.dynamic_update_slice_in_dim(
+                m_next, val2, (b_next - kk) % arr_out * clean, axis=1
+            )
+            if kk < arr_out - y2:
+                block_last = jax.lax.ppermute(block_last, net_axis, leaves)
+                m_next = lax.dynamic_update_slice_in_dim(
+                    m_next, block_last, (b_next + kk) % arr_out * clean, axis=1
+                )
+            kk = kk + 1
+        return m_next
+
+    piece = _post_trees(stacked, net_axis="ha")
     gate_part = jnp.dot(piece[0], w_gate, preferred_element_type=jnp.float32)
     up_part = jnp.dot(piece[0], w_up, preferred_element_type=jnp.float32)
     back_part = lax.dot_general(

time: 385 us -> 414 us (1.075)
  starting transfers between devices: 14.9 us -> 64.2 us
  blocking collectives: 195 us -> 169 us
    ppermute x0 -> x15, starting transfers between devices: none -> 48.8 us  [the longest x7 33.5 us: _post_trees(): block_last = jax.lax.ppermute(block_last, net_axis, leaves)]
    all_gather x1 -> x0, blocking collectives: 25.4 us -> none  [local(): piece = lax.all_gather(stacked, 'ha', axis=1, tiled=True)]
  transfers between devices with their start and end apart: 5 -> 20, of which waited for: 1 -> 1; matrix products, arithmetic and copies ran while one was open for 0% -> 1% of each run, Pallas kernels for 0% -> 0%
where the time goes in v1:
time: 414 us; the launch traced here: 413 us
  blocking collectives  169 us (41%)
  waiting for transfers between devices  143 us (35%)
  starting transfers between devices  64.2 us (16%)
  between operations  15 us (4%)
  matrix products  9.35 us (2%)
  other arithmetic  6.11 us (1%)
  local copies, waits for them, and re-layouts  5.95 us (1%)
    psum x1, waiting for transfers between devices, local(): summed = lax.psum(partial_sums, 'wa')  143 us
    psum x1, blocking collectives, local(): row_dot = lax.psum(jnp.sum(scaled * stream, axis=1), 'wa')[:, None]  70.7 us
    psum x1, blocking collectives, local(): squares = lax.psum(jnp.sum(stream * stream, axis=1), 'wa')  68.9 us
    ppermute x7, starting transfers between devices, _post_trees(): block_last = jax.lax.ppermute(block_last, net_axis, leaves)  33.5 us
    unnamed x1, blocking collectives  29.3 us
    ppermute x8, starting transfers between devices, _post_trees(): val2 = jax.lax.ppermute(val2, net_axis, chunks)  15.4 us
    unnamed x4, starting transfers between devices  15.3 us
  transfers between devices with their start and end apart: 20, of which 1 were waited for; matrix products, arithmetic and copies ran while one was open for 1% of the time, Pallas kernels for 0%

profile of v1, /device:TPU:1, one launch (start us, length us, event | category | flops | bytes accessed | tf_op | source)
XLA Modules:
  0.0 412.8 jit_solution(1080212750354283671)
XLA Ops:
  7.5 68.9 %psum.21 = f32[12]{0:T(128)S(1)} all-reduce(f32[12]{0:T(128)S(1)} %fusion.8), channel_id=1, replica_groups=mesh['wa'=32,'ha'=16] {'wa'}, use_global_device_ids=true, to_apply=%region_1.0 | all-reduce | flops 12 | bytes 96 | tf_op jit(solution)/shard_map/psum | solution.py:18
  80.5 6.0 %collective-permute-start.1 = (bf16[2,12,512]{2,1,0:T(8,128)(2,1)S(1)}, bf16[2,12,512]{2,1,0:T(8,128)(2,1)S(1)}, u32[]{:S(2)}, u32[]{:S(2)}) collective-permute-start(bf16[2,12,512]{2,1,0:T(8,128)(2,1)S(1)} %pad_maximum_fusion.1), channel_id=1, source_target_pairs={{0,15},{1,0},{2,1},{3,2},{4,3},{5,4},{6,5},{7,6},{8,7},{9,8},{10,9... | collective-permute-start | bytes 73736 | tf_op jit(solution)/shard_map/ppermute | solution.py:49
  86.5 1.9 collective-permute-start.2
  88.5 4.6 %collective-permute-start.3 = (bf16[2,12,512]{2,1,0:T(8,128)(2,1)S(1)}, bf16[2,12,512]{2,1,0:T(8,128)(2,1)S(1)}, u32[]{:S(2)}, u32[]{:S(2)}) collective-permute-start(bf16[2,12,512]{2,1,0:T(8,128)(2,1)S(1)} %collective-permute-done.1), channel_id=1, source_target_pairs={{0,15},{1,0},{2,1},{3,2},{4,3},{5,4},{6,5},{7,6},{8,7},{9,8},{10,9... | collective-permute-start | bytes 73736 | tf_op jit(solution)/shard_map/ppermute | solution.py:49
  93.1 1.9 collective-permute-start.4
  95.0 4.6 %collective-permute-start.5 = (bf16[2,12,512]{2,1,0:T(8,128)(2,1)S(1)}, bf16[2,12,512]{2,1,0:T(8,128)(2,1)S(1)}, u32[]{:S(2)}, u32[]{:S(2)}) collective-permute-start(bf16[2,12,512]{2,1,0:T(8,128)(2,1)S(1)} %collective-permute-done.3), channel_id=1, source_target_pairs={{0,15},{1,0},{2,1},{3,2},{4,3},{5,4},{6,5},{7,6},{8,7},{9,8},{10,9... | collective-permute-start | bytes 73736 | tf_op jit(solution)/shard_map/ppermute | solution.py:49
  99.6 1.9 collective-permute-start.6
  101.5 4.6 %collective-permute-start.7 = (bf16[2,12,512]{2,1,0:T(8,128)(2,1)S(1)}, bf16[2,12,512]{2,1,0:T(8,128)(2,1)S(1)}, u32[]{:S(2)}, u32[]{:S(2)}) collective-permute-start(bf16[2,12,512]{2,1,0:T(8,128)(2,1)S(1)} %collective-permute-done.5), channel_id=1, source_target_pairs={{0,15},{1,0},{2,1},{3,2},{4,3},{5,4},{6,5},{7,6},{8,7},{9,8},{10,9... | collective-permute-start | bytes 73736 | tf_op jit(solution)/shard_map/ppermute | solution.py:49
  106.1 1.9 collective-permute-start.8
  108.1 4.6 %collective-permute-start.9 = (bf16[2,12,512]{2,1,0:T(8,128)(2,1)S(1)}, bf16[2,12,512]{2,1,0:T(8,128)(2,1)S(1)}, u32[]{:S(2)}, u32[]{:S(2)}) collective-permute-start(bf16[2,12,512]{2,1,0:T(8,128)(2,1)S(1)} %collective-permute-done.7), channel_id=1, source_target_pairs={{0,15},{1,0},{2,1},{3,2},{4,3},{5,4},{6,5},{7,6},{8,7},{9,8},{10,9... | collective-permute-start | bytes 73736 | tf_op jit(solution)/shard_map/ppermute | solution.py:49
  112.7 1.9 collective-permute-start.10
  114.6 4.6 %collective-permute-start.11 = (bf16[2,12,512]{2,1,0:T(8,128)(2,1)S(1)}, bf16[2,12,512]{2,1,0:T(8,128)(2,1)S(1)}, u32[]{:S(2)}, u32[]{:S(2)}) collective-permute-start(bf16[2,12,512]{2,1,0:T(8,128)(2,1)S(1)} %collective-permute-done.9), channel_id=1, source_target_pairs={{0,15},{1,0},{2,1},{3,2},{4,3},{5,4},{6,5},{7,6},{8,7},{9,8},{10,9... | collective-permute-start | bytes 73736 | tf_op jit(solution)/shard_map/ppermute | solution.py:49
  119.2 1.9 collective-permute-start.12
  121.1 4.6 %collective-permute-start.13 = (bf16[2,12,512]{2,1,0:T(8,128)(2,1)S(1)}, bf16[2,12,512]{2,1,0:T(8,128)(2,1)S(1)}, u32[]{:S(2)}, u32[]{:S(2)}) collective-permute-start(bf16[2,12,512]{2,1,0:T(8,128)(2,1)S(1)} %collective-permute-done.11), channel_id=1, source_target_pairs={{0,15},{1,0},{2,1},{3,2},{4,3},{5,4},{6,5},{7,6},{8,7},{9,8},{10,9... | collective-permute-start | bytes 73736 | tf_op jit(solution)/shard_map/ppermute | solution.py:49
  132.3 2.3 convolution_bitcast_fusion
  135.7 2.1 pad_maximum_fusion
  137.9 143.4 %all-reduce.4.cloned.1.call-done = f32[3,192,1664]{2,1,0:T(8,128)} async-done(((f32[3,192,1664]{2,1,0:T(8,128)}), f32[3,192,1664]{2,1,0:T(8,128)}) %all-reduce.4.cloned.1.call-update) | async-done | bytes 3833872 | tf_op jit(solution)/shard_map/psum | solution.py:63
  281.3 2.8 fusion.6
  284.1 3.2 convolution_add_fusion
  287.3 29.3 %fusion = f32[16,512]{1,0:T(8,128)S(1)} fusion(f32[192,512]{1,0:T(8,128)} %convolution_add_fusion), kind=kCustom, calls=%all-reduce-scatter | all-reduce-scatter fusion | flops 131073 | bytes 428032
  318.1 2.9 collective-permute-start.16
  321.0 5.6 %collective-permute-start.17 = (f32[16,512]{1,0:T(8,128)S(1)}, f32[16,512]{1,0:T(8,128)S(1)}, u32[]{:S(2)}, u32[]{:S(2)}) collective-permute-start(f32[16,512]{1,0:T(8,128)S(1)} %fusion), channel_id=1, source_target_pairs={{0,3},{1,4},{2,5},{3,6},{4,7},{5,8},{6,9},{7,10},{8,11},{9,12},{10... | collective-permute-start | bytes 98312
  326.7 5.2 %collective-permute-start.18 = (f32[12,512]{1,0:T(8,128)S(1)}, f32[12,512]{1,0:T(8,128)S(1)}, u32[]{:S(2)}, u32[]{:S(2)}) collective-permute-start(f32[12,512]{1,0:T(8,128)S(1)} %slice.26), channel_id=1, source_target_pairs={{0,4},{1,5},{2,6},{3,7},{4,8},{5,9},{6,10},{7,11},{8,12},{9,13},{1... | collective-permute-start | bytes 73736
  334.5 70.7 %psum.23 = f32[12]{0:T(128)S(1)} all-reduce(f32[12]{0:T(128)S(1)} %fusion.15), channel_id=1, replica_groups=mesh['wa'=32,'ha'=16] {'wa'}, use_global_device_ids=true, to_apply=%region_5.6 | all-reduce | flops 12 | bytes 96 | tf_op jit(solution)/shard_map/psum | solution.py:78
  (63 shorter events, 16.5 us)
Async XLA Ops:
  6.5 128.6 %copy-start = (bf16[512,1664]{1,0:T(8,128)(2,1)S(1)}, bf16[512,1664]{1,0:T(8,128)(2,1)}, u32[]{:S(2)}) copy-start(bf16[512,1664]{1,0:T(8,128)(2,1)} %param.9) | copy-start | bytes 5111812
  6.5 274.7 %all-reduce.4.cloned.1.call-start = ((), (), s32[]{:S(2)}) async-start(), calls=%async_computation | async-start | bytes 7667712 | tf_op jit(solution)/shard_map/psum | solution.py:63
  78.6 8.0 %collective-permute-start = (bf16[2,12,512]{2,1,0:T(8,128)(2,1)S(1)}, bf16[2,12,512]{2,1,0:T(8,128)(2,1)S(1)}, u32[]{:S(2)}, u32[]{:S(2)}) collective-permute-start(bf16[2,12,512]{2,1,0:T(8,128)(2,1)S(1)} %pad_maximum_fusion.1), channel_id=1, source_target_pairs={{0,1},{1,2},{2,3},{3,4},{4,5},{5,6},{6,7},{7,8},{8,9},{9,10},{10,1... | collective-permute-start | bytes 73736 | tf_op jit(solution)/shard_map/ppermute | solution.py:44
  80.5 8.0 %collective-permute-start.1 = (bf16[2,12,512]{2,1,0:T(8,128)(2,1)S(1)}, bf16[2,12,512]{2,1,0:T(8,128)(2,1)S(1)}, u32[]{:S(2)}, u32[]{:S(2)}) collective-permute-start(bf16[2,12,512]{2,1,0:T(8,128)(2,1)S(1)} %pad_maximum_fusion.1), channel_id=1, source_target_pairs={{0,15},{1,0},{2,1},{3,2},{4,3},{5,4},{6,5},{7,6},{8,7},{9,8},{10,9... | collective-permute-start | bytes 73736 | tf_op jit(solution)/shard_map/ppermute | solution.py:49
  86.5 6.5 %collective-permute-start.2 = (bf16[2,12,512]{2,1,0:T(8,128)(2,1)S(1)}, bf16[2,12,512]{2,1,0:T(8,128)(2,1)S(1)}, u32[]{:S(2)}, u32[]{:S(2)}) collective-permute-start(bf16[2,12,512]{2,1,0:T(8,128)(2,1)S(1)} %collective-permute-done), channel_id=1, source_target_pairs={{0,1},{1,2},{2,3},{3,4},{4,5},{5,6},{6,7},{7,8},{8,9},{9,10},{10,1... | collective-permute-start | bytes 73736 | tf_op jit(solution)/shard_map/ppermute | solution.py:44
  88.5 6.5 %collective-permute-start.3 = (bf16[2,12,512]{2,1,0:T(8,128)(2,1)S(1)}, bf16[2,12,512]{2,1,0:T(8,128)(2,1)S(1)}, u32[]{:S(2)}, u32[]{:S(2)}) collective-permute-start(bf16[2,12,512]{2,1,0:T(8,128)(2,1)S(1)} %collective-permute-done.1), channel_id=1, source_target_pairs={{0,15},{1,0},{2,1},{3,2},{4,3},{5,4},{6,5},{7,6},{8,7},{9,8},{10,9... | collective-permute-start | bytes 73736 | tf_op jit(solution)/shard_map/ppermute | solution.py:49
  93.1 6.5 %collective-permute-start.4 = (bf16[2,12,512]{2,1,0:T(8,128)(2,1)S(1)}, bf16[2,12,512]{2,1,0:T(8,128)(2,1)S(1)}, u32[]{:S(2)}, u32[]{:S(2)}) collective-permute-start(bf16[2,12,512]{2,1,0:T(8,128)(2,1)S(1)} %collective-permute-done.2), channel_id=1, source_target_pairs={{0,1},{1,2},{2,3},{3,4},{4,5},{5,6},{6,7},{7,8},{8,9},{9,10},{10,1... | collective-permute-start | bytes 73736 | tf_op jit(solution)/shard_map/ppermute | solution.py:44
  95.0 6.5 %collective-permute-start.5 = (bf16[2,12,512]{2,1,0:T(8,128)(2,1)S(1)}, bf16[2,12,512]{2,1,0:T(8,128)(2,1)S(1)}, u32[]{:S(2)}, u32[]{:S(2)}) collective-permute-start(bf16[2,12,512]{2,1,0:T(8,128)(2,1)S(1)} %collective-permute-done.3), channel_id=1, source_target_pairs={{0,15},{1,0},{2,1},{3,2},{4,3},{5,4},{6,5},{7,6},{8,7},{9,8},{10,9... | collective-permute-start | bytes 73736 | tf_op jit(solution)/shard_map/ppermute | solution.py:49
  99.6 6.5 %collective-permute-start.6 = (bf16[2,12,512]{2,1,0:T(8,128)(2,1)S(1)}, bf16[2,12,512]{2,1,0:T(8,128)(2,1)S(1)}, u32[]{:S(2)}, u32[]{:S(2)}) collective-permute-start(bf16[2,12,512]{2,1,0:T(8,128)(2,1)S(1)} %collective-permute-done.4), channel_id=1, source_target_pairs={{0,1},{1,2},{2,3},{3,4},{4,5},{5,6},{6,7},{7,8},{8,9},{9,10},{10,1... | collective-permute-start | bytes 73736 | tf_op jit(solution)/shard_map/ppermute | solution.py:44
  101.5 6.5 %collective-permute-start.7 = (bf16[2,12,512]{2,1,0:T(8,128)(2,1)S(1)}, bf16[2,12,512]{2,1,0:T(8,128)(2,1)S(1)}, u32[]{:S(2)}, u32[]{:S(2)}) collective-permute-start(bf16[2,12,512]{2,1,0:T(8,128)(2,1)S(1)} %collective-permute-done.5), channel_id=1, source_target_pairs={{0,15},{1,0},{2,1},{3,2},{4,3},{5,4},{6,5},{7,6},{8,7},{9,8},{10,9... | collective-permute-start | bytes 73736 | tf_op jit(solution)/shard_map/ppermute | solution.py:49
  106.1 6.5 %collective-permute-start.8 = (bf16[2,12,512]{2,1,0:T(8,128)(2,1)S(1)}, bf16[2,12,512]{2,1,0:T(8,128)(2,1)S(1)}, u32[]{:S(2)}, u32[]{:S(2)}) collective-permute-start(bf16[2,12,512]{2,1,0:T(8,128)(2,1)S(1)} %collective-permute-done.6), channel_id=1, source_target_pairs={{0,1},{1,2},{2,3},{3,4},{4,5},{5,6},{6,7},{7,8},{8,9},{9,10},{10,1... | collective-permute-start | bytes 73736 | tf_op jit(solution)/shard_map/ppermute | solution.py:44
  108.1 6.5 %collective-permute-start.9 = (bf16[2,12,512]{2,1,0:T(8,128)(2,1)S(1)}, bf16[2,12,512]{2,1,0:T(8,128)(2,1)S(1)}, u32[]{:S(2)}, u32[]{:S(2)}) collective-permute-start(bf16[2,12,512]{2,1,0:T(8,128)(2,1)S(1)} %collective-permute-done.7), channel_id=1, source_target_pairs={{0,15},{1,0},{2,1},{3,2},{4,3},{5,4},{6,5},{7,6},{8,7},{9,8},{10,9... | collective-permute-start | bytes 73736 | tf_op jit(solution)/shard_map/ppermute | solution.py:49
  112.7 6.5 %collective-permute-start.10 = (bf16[2,12,512]{2,1,0:T(8,128)(2,1)S(1)}, bf16[2,12,512]{2,1,0:T(8,128)(2,1)S(1)}, u32[]{:S(2)}, u32[]{:S(2)}) collective-permute-start(bf16[2,12,512]{2,1,0:T(8,128)(2,1)S(1)} %collective-permute-done.8), channel_id=1, source_target_pairs={{0,1},{1,2},{2,3},{3,4},{4,5},{5,6},{6,7},{7,8},{8,9},{9,10},{10,1... | collective-permute-start | bytes 73736 | tf_op jit(solution)/shard_map/ppermute | solution.py:44
  114.6 6.5 %collective-permute-start.11 = (bf16[2,12,512]{2,1,0:T(8,128)(2,1)S(1)}, bf16[2,12,512]{2,1,0:T(8,128)(2,1)S(1)}, u32[]{:S(2)}, u32[]{:S(2)}) collective-permute-start(bf16[2,12,512]{2,1,0:T(8,128)(2,1)S(1)} %collective-permute-done.9), channel_id=1, source_target_pairs={{0,15},{1,0},{2,1},{3,2},{4,3},{5,4},{6,5},{7,6},{8,7},{9,8},{10,9... | collective-permute-start | bytes 73736 | tf_op jit(solution)/shard_map/ppermute | solution.py:49
  119.2 6.5 %collective-permute-start.12 = (bf16[2,12,512]{2,1,0:T(8,128)(2,1)S(1)}, bf16[2,12,512]{2,1,0:T(8,128)(2,1)S(1)}, u32[]{:S(2)}, u32[]{:S(2)}) collective-permute-start(bf16[2,12,512]{2,1,0:T(8,128)(2,1)S(1)} %collective-permute-done.10), channel_id=1, source_target_pairs={{0,1},{1,2},{2,3},{3,4},{4,5},{5,6},{6,7},{7,8},{8,9},{9,10},{10,1... | collective-permute-start | bytes 73736 | tf_op jit(solution)/shard_map/ppermute | solution.py:44
  121.1 10.6 %collective-permute-start.13 = (bf16[2,12,512]{2,1,0:T(8,128)(2,1)S(1)}, bf16[2,12,512]{2,1,0:T(8,128)(2,1)S(1)}, u32[]{:S(2)}, u32[]{:S(2)}) collective-permute-start(bf16[2,12,512]{2,1,0:T(8,128)(2,1)S(1)} %collective-permute-done.11), channel_id=1, source_target_pairs={{0,15},{1,0},{2,1},{3,2},{4,3},{5,4},{6,5},{7,6},{8,7},{9,8},{10,9... | collective-permute-start | bytes 73736 | tf_op jit(solution)/shard_map/ppermute | solution.py:49
  125.7 6.3 %collective-permute-start.14 = (bf16[2,12,512]{2,1,0:T(8,128)(2,1)S(1)}, bf16[2,12,512]{2,1,0:T(8,128)(2,1)S(1)}, u32[]{:S(2)}, u32[]{:S(2)}) collective-permute-start(bf16[2,12,512]{2,1,0:T(8,128)(2,1)S(1)} %collective-permute-done.12), channel_id=1, source_target_pairs={{0,1},{1,2},{2,3},{3,4},{4,5},{5,6},{6,7},{7,8},{8,9},{9,10},{10,1... | collective-permute-start | bytes 73736 | tf_op jit(solution)/shard_map/ppermute | solution.py:44
  137.9 146.2 %copy-start.2 = (bf16[512,1664]{1,0:T(8,128)(2,1)S(1)}, bf16[512,1664]{1,0:T(8,128)(2,1)}, u32[]{:S(2)}) copy-start(bf16[512,1664]{1,0:T(8,128)(2,1)} %param.10) | copy-start | bytes 5111812
  284.1 50.3 %copy-start.3 = (bf16[12,512]{1,0:T(8,128)(2,1)S(1)}, bf16[12,512]{1,0:T(8,128)(2,1)}, u32[]{:S(2)}) copy-start(bf16[12,512]{1,0:T(8,128)(2,1)} %param.6) | copy-start | bytes 36868
  284.1 121.2 %copy-start.4 = (bf16[12,512]{1,0:T(8,128)(2,1)S(1)}, bf16[12,512]{1,0:T(8,128)(2,1)}, u32[]{:S(2)}) copy-start(bf16[12,512]{1,0:T(8,128)(2,1)} %param.7) | copy-start | bytes 36868
  316.5 17.3 %collective-permute-start.15 = (f32[16,512]{1,0:T(8,128)S(1)}, f32[16,512]{1,0:T(8,128)S(1)}, u32[]{:S(2)}, u32[]{:S(2)}) collective-permute-start(f32[16,512]{1,0:T(8,128)S(1)} %fusion), channel_id=1, source_target_pairs={{0,1},{1,2},{2,3},{3,4},{4,5},{5,6},{6,7},{7,8},{8,9},{9,10},{10,1... | collective-permute-start | bytes 98312
  318.1 15.7 %collective-permute-start.16 = (f32[16,512]{1,0:T(8,128)S(1)}, f32[16,512]{1,0:T(8,128)S(1)}, u32[]{:S(2)}, u32[]{:S(2)}) collective-permute-start(f32[16,512]{1,0:T(8,128)S(1)} %fusion), channel_id=1, source_target_pairs={{0,2},{1,3},{2,4},{3,5},{4,6},{5,7},{6,8},{7,9},{8,10},{9,11},{10,... | collective-permute-start | bytes 98312
  321.0 12.8 %collective-permute-start.17 = (f32[16,512]{1,0:T(8,128)S(1)}, f32[16,512]{1,0:T(8,128)S(1)}, u32[]{:S(2)}, u32[]{:S(2)}) collective-permute-start(f32[16,512]{1,0:T(8,128)S(1)} %fusion), channel_id=1, source_target_pairs={{0,3},{1,4},{2,5},{3,6},{4,7},{5,8},{6,9},{7,10},{8,11},{9,12},{10... | collective-permute-start | bytes 98312
  326.7 7.2 %collective-permute-start.18 = (f32[12,512]{1,0:T(8,128)S(1)}, f32[12,512]{1,0:T(8,128)S(1)}, u32[]{:S(2)}, u32[]{:S(2)}) collective-permute-start(f32[12,512]{1,0:T(8,128)S(1)} %slice.26), channel_id=1, source_target_pairs={{0,4},{1,5},{2,6},{3,7},{4,8},{5,9},{6,10},{7,11},{8,12},{9,13},{1... | collective-permute-start | bytes 73736
  (1 other events, 2.3 us)
Sparse Core Ops, SparseCore 0:
  138.0 143.2 all-reduce.3
